TPU v7x, 256 devices: a whole 4x4x8 slice. The times are simulated.
256 devices in a mesh: blk: 64 (over z, x, core), head: 2 (over y_hi), dec: 2 (over y_lo).
Axes of the slice: x: 4, y: 4 (y_hi: 2, y_lo: 2; y = y_hi * 2 + y_lo), z: 8, core: 2. Of those that a mesh axis runs over, the one named last changes fastest.
Arguments:
- queries: bfloat16 [16384, 1536], P('blk', ('head', 'dec')), may hold values from -12 to 12
- key_vectors: bfloat16 [16384, 1536], P('blk', ('head', 'dec')), may hold values from -5 to 5
- values: bfloat16 [16384, 1536], P('blk', ('head', 'dec')), may hold values from -6 to 6
- lookback: int32 [12], replicated, may hold values from 0 to 5, as said below
- residual: bfloat16 [16384, 3072], P(('blk', 'head', 'dec')), may hold values from -0.1875 to 0.1875
- out_weight: bfloat16 [1536, 3072], P(('head', 'dec')), may hold values from -0.15625 to 0.15625
- branch_gate: float32 [3072], replicated, may hold values from 0.5 to 1.5
- final_shift: float32 [3072], replicated, may hold values from -0.5 to 0.5
- final_scale: float32 [3072], replicated, may hold values from -0.5 to 0.5
- final_weight: bfloat16 [3072, 64], replicated, may hold values from -0.109375 to 0.109375
- decoder_kernel: bfloat16 [432, 512], replicated, may hold values from -0.3125 to 0.3125
- decoder_bias: float32 [512], replicated, may hold values from -3 to 3
Outputs:
- features: bfloat16 [1024, 64, 512], P(('blk', 'head', 'dec'))
Inputs may be any that keep to these rules, and one draw needn't show every extreme that they name: lookback[h] is how many frames before its own the queries of head h may see; some head sees 5 earlier frames and some head none.
All inputs are finite; a program needn't handle non-finite values.
Results may differ from a plain program's by a relative error of at most 0.02.
Values may be sent and summed in bfloat16 or wider, within the bound.
No kernel may reach another device: no remote copies, remote signals or barrier semaphores. Data moves between devices by JAX's collectives and lax.ppermute only.
A program may use at most 192 MiB of HBM per device.

v0:
```python
import jax
import jax.numpy as jnp
from jax import lax
from jax.sharding import PartitionSpec as P

DH = 128
LC = 16
FRAMES = 8
PW = 32


def padded_2(cells, sides, width):
    for axis, dim in sides:
        count = lax.axis_size(axis)
        ends = count - 1
        head = lax.slice_in_dim(cells, 0, width, axis=dim)
        tail = lax.slice_in_dim(cells, cells.shape[dim] - width, cells.shape[dim], axis=dim)
        cells = jnp.concatenate(
            [
                lax.ppermute(tail, axis, [(i, (i + 1) % count) for i in range(ends)]),
                cells,
                lax.ppermute(head, axis, [((i + 1) % count, i) for i in range(ends)]),
            ],
            axis=dim,
        )
    return cells


def from_behind(x, axis, by):
    peers = lax.axis_size(axis)
    pairs = [(i, i + by) for i in range(peers) if 0 <= i + by < peers]
    return lax.ppermute(x, axis, pairs)


def attend_block(carry, shard_pair, query_heads, query_frame, lookback_heads, frame_len):
    running_max, row_total, accumulated = carry
    key_block, value_block = shard_pair
    key_count = key_block.shape[0]
    head_count = query_heads.shape[1]
    key_heads = key_block.reshape(key_count, head_count, DH)
    value_heads = value_block.reshape(key_count, head_count, DH)
    scores = jnp.einsum(
        "qhd,khd->hqk", query_heads, key_heads, preferred_element_type=jnp.float32
    ) * DH ** (-0.5)
    key_pos = jnp.arange(key_count, dtype=jnp.int32)
    key_frame = key_pos // frame_len
    visible = (
        (key_pos >= 0)[None, None, :]
        & (key_frame[None, None, :] <= query_frame[None, :, None])
        & (key_frame[None, None, :] >= query_frame[None, :, None] - lookback_heads[:, None, None])
    )
    masked = jnp.where(visible, scores, -1e30)
    newest_max = jnp.maximum(running_max, jnp.max(masked, axis=2))
    weights = jnp.where(visible, jnp.exp(scores - newest_max[:, :, None]), 0.0).astype(jnp.bfloat16)
    row_total = jnp.sum(weights.astype(jnp.float32), axis=2)
    accumulated = jnp.einsum(
        "hqk,khd->hqd", weights, value_heads, preferred_element_type=jnp.float32
    )
    return (newest_max, row_total, accumulated)


def per_device(
    queries,
    key_vectors,
    values,
    lookback,
    residual,
    out_weight,
    branch_gate,
    final_shift,
    final_scale,
    final_weight,
    decoder_kernel,
    decoder_bias,
):
    slab_rows = queries.shape[0]
    head_count = queries.shape[1] // DH
    blocks = lax.axis_size("blk")
    block_index = lax.axis_index("blk")
    frame_len = slab_rows * blocks // FRAMES
    query_heads = queries.reshape(slab_rows, head_count, DH)
    query_frame = (block_index * slab_rows + jnp.arange(slab_rows, dtype=jnp.int32)) // frame_len
    lookback_heads = lax.dynamic_slice_in_dim(
        lookback, lax.axis_index(("head", "dec")) * head_count, head_count
    )
    initial = (
        jnp.full((head_count, slab_rows), -1e30, jnp.float32),
        jnp.zeros((head_count, slab_rows), jnp.float32),
        jnp.zeros((head_count, slab_rows, DH), jnp.float32),
    )
    carry = attend_block(
        initial,
        (
            lax.all_gather(key_vectors, "blk", axis=0, tiled=True),
            lax.all_gather(values, "blk", axis=0, tiled=True),
        ),
        query_heads,
        query_frame,
        lookback_heads,
        frame_len,
    )
    newest_max, row_total, accumulated = carry
    attended = (
        (accumulated / row_total[:, :, None])
        .transpose(1, 0, 2)
        .reshape(slab_rows, head_count * DH)
        .astype(jnp.bfloat16)
    )
    tokens_dev = slab_rows // lax.axis_size(("head", "dec"))
    projected = lax.psum_scatter(
        jnp.dot(attended, out_weight, preferred_element_type=jnp.float32).astype(jnp.bfloat16),
        ("head", "dec"),
        scatter_dimension=0,
        tiled=True,
    ).astype(jnp.float32)
    hidden = residual.astype(jnp.float32) + branch_gate[None, :] * projected
    center = jnp.mean(hidden, axis=1, keepdims=True)
    spread = jnp.mean((hidden - center) ** 2, axis=1, keepdims=True)
    normed = (
        (hidden - center) * lax.rsqrt(spread + 1e-06) * (1.0 + final_scale[None, :])
        + final_shift[None, :]
    ).astype(jnp.bfloat16)
    patches = jnp.dot(normed, final_weight, preferred_element_type=jnp.float32).astype(jnp.bfloat16)
    patch_rows = tokens_dev // PW
    tile_rows = 2 * patch_rows
    width = 2 * PW
    tile = (
        patches.reshape(patch_rows, PW, 2, 2, LC)
        .transpose(0, 2, 1, 3, 4)
        .reshape(tile_rows, width * LC)
    )
    padded = padded_2(tile, ((("blk", "head", "dec"), 0),), 1)
    frame_stride = blocks // FRAMES
    frame_index = block_index // frame_stride
    prior_one = from_behind(padded, "blk", frame_stride)
    prior_one = jnp.where(frame_index >= 1, prior_one, padded)
    prior_two = from_behind(prior_one, "blk", frame_stride)
    prior_two = jnp.where(frame_index >= 1, prior_two, padded)
    history = jnp.stack([prior_two, prior_one, padded]).reshape(3, tile_rows + 2, width, LC)
    history = jnp.pad(history, ((0, 0), (0, 0), (1, 1), (0, 0)))
    windows = [
        history[time_tap, row_tap : row_tap + tile_rows, column_tap : column_tap + width, :]
        for time_tap in range(3)
        for row_tap in range(3)
        for column_tap in range(3)
    ]
    columns = jnp.concatenate(windows, axis=-1).reshape(tile_rows * width, 27 * LC)
    summed = (
        jnp.dot(columns, decoder_kernel, preferred_element_type=jnp.float32) + decoder_bias[None, :]
    )
    return summed.astype(jnp.bfloat16).reshape(tile_rows, width, decoder_kernel.shape[1])


def solution(mesh):
    in_specs = (
        P("blk", ("head", "dec")),
        P("blk", ("head", "dec")),
        P("blk", ("head", "dec")),
        P(),
        P(("blk", "head", "dec"), None),
        P(("head", "dec"), None),
        P(),
        P(),
        P(),
        P(),
        P(),
        P(),
    )
    out_specs = P(("blk", "head", "dec"), None, None)
    return jax.shard_map(
        per_device, mesh=mesh, in_specs=in_specs, out_specs=out_specs, check_vma=False
    )
```

profile of v0, /device:TPU:128, one launch (start us, length us, event | category | flops | bytes accessed | tf_op | source)
XLA Modules:
  0.0 315.5 jit_solution(12404184327450962504)
XLA Ops:
  6.5 1.9 copy.25
  9.3 1.1 copy.24
  10.3 0.7 dynamic_slice.3
  11.2 4.4 %broadcast_compare_fusion = pred[256,16384]{1,0:T(8,128)(4,1)} fusion(s32[16384]{0:T(1024)S(1)} %add_select_fusion, s32[256]{0:T(256)S(1)} %and_select_fusion), kind=kLoop, calls=%fused_computation.4 | loop fusion | flops 4194304 | bytes 4260864 | tf_op jit(solution)/shard_map/le | solution.py:49
  15.5 87.7 %all-gather.3.cloned.1.call-done = bf16[16384,384]{0,1:T(8,128)(2,1)} async-done(((bf16[256,384]{0,1:T(8,128)(2,1)}), bf16[16384,384]{0,1:T(8,128)(2,1)}) %all-gather.3.cloned.1.call-update) | async-done | bytes 12582928 | tf_op jit(solution)/shard_map/all_gather | solution.py:94
  103.3 28.9 %select_reduce_fusion = (f32[3,256]{1,0:T(4,128)S(1)}, f32[3,256,16384]{2,1,0:T(8,128)}) fusion(s32[3,256]{1,0:T(4,128)S(1)} %broadcast_subtract_fusion, s32[16384]{0:T(1024)S(1)} %add_select_fusion, pred[256,16384]{1,0:T(8,128)(4,1)} %broadcast_compare_fusion, bf16[256,3,128]{0,2,1:T(8,128)(2,1)S(1)} %bitcast.81, bf16[16384,3,128]{0,2,1:T(8,128)(2,1)} %bitcast.84), kind=kOutput, calls=%fused_computation.2 | convolution fusion | flops 3284139264 | bytes 67377152 | tf_op jit(solution)/shard_map/qhd,khd->hqk/dot_general | solution.py:42
  132.2 25.4 %convert_reduce_fusion = f32[3,256]{1,0:T(4,128)S(1)} fusion(f32[3,256]{1,0:T(4,128)S(1)} %broadcast_maximum_fusion, f32[3,256,16384]{2,1,0:T(8,128)} %get-tuple-element.34, s32[3,256]{1,0:T(4,128)S(1)} %broadcast_subtract_fusion, s32[16384]{0:T(1024)S(1)} %add_select_fusion, pred[256,16384]{1,0:T(8,128)(4,1)} %broadcast_compare_fusion), kind=kLoop, calls=%fused_computation | loop fusion | flops 100662528 | bytes 54600704 | tf_op jit(solution)/shard_map/reduce_sum | solution.py:55
  157.6 38.9 %all-gather.5.cloned.1.call-done = bf16[16384,384]{1,0:T(8,128)(2,1)} async-done(((bf16[256,384]{1,0:T(8,128)(2,1)}), bf16[16384,384]{1,0:T(8,128)(2,1)}) %all-gather.5.cloned.1.call-update) | async-done | bytes 12582928 | tf_op jit(solution)/shard_map/all_gather | solution.py:95
  196.5 16.7 %copy.28 = bf16[16384,384]{0,1:T(8,128)(2,1)} copy(bf16[16384,384]{1,0:T(8,128)(2,1)} %all-gather.5.cloned.1.call-done) | data formatting | bytes 25165824 | tf_op jit(solution)/shard_map/all_gather | solution.py:95
  213.3 24.8 %fusion.2 = bf16[256,3,128]{0,2,1:T(8,128)(2,1)S(1)} fusion(bf16[16384,3,128]{0,2,1:T(8,128)(2,1)} %bitcast.51, f32[256,3]{0,1:T(4,128)S(1)} %bitcast.83, f32[3,256,16384]{2,1,0:T(8,128)} %get-tuple-element.34, f32[3,256]{1,0:T(4,128)S(1)} %broadcast_maximum_fusion, s32[3,256]{1,0:T(4,128)S(1)} %broadcast_subtract_fusion, s32[16384]{0:T(1024)S(1)} %add_select_fusion, ...), kind=kOutput, calls=%fused_computation.10 | convolution fusion | flops 3296919552 | bytes 67380224 | tf_op jit(solution)/shard_map/hqk,khd->hqd/dot_general | solution.py:56
  238.1 2.2 convolution_convert_fusion
  240.3 28.1 %reduce-scatter.2.cloned.1.call-done = bf16[64,3072]{1,0:T(8,128)(2,1)} async-done(((bf16[256,3072]{1,0:T(8,128)(2,1)}), bf16[64,3072]{1,0:T(8,128)(2,1)}) %reduce-scatter.2.cloned.1.call-update) | async-done | bytes 393232 | tf_op jit(solution)/shard_map/reduce_scatter | solution.py:110
  268.4 1.2 fusion.3
  269.7 1.3 multiply_reduce_fusion
  271.0 1.4 convolution_convert_fusion.1
  272.8 2.2 collective-permute-start
  275.1 8.7 %collective-permute-start.1 = (bf16[1,1024]{1,0:T(2,128)(2,1)S(1)}, bf16[1,1024]{1,0:T(2,128)(2,1)S(1)}, u32[]{:S(2)}, u32[]{:S(2)}) collective-permute-start(bf16[1,1024]{1,0:T(2,128)(2,1)S(1)} %get-tuple-element.32), channel_id=1, source_target_pairs={{1,0},{2,1},{3,2},{4,3},{5,4},{6,5},{7,6},{8,7},{9,8},{10,9},{11,1... | collective-permute-start | bytes 6152 | tf_op jit(solution)/shard_map/ppermute | solution.py:22
  284.1 1.0 collective-permute-done.1
  285.4 1.9 collective-permute-start.2
  287.5 4.7 %collective-permute-done.2 = bf16[6,1024]{1,0:T(8,128)(2,1)S(1)} collective-permute-done((bf16[6,1024]{1,0:T(8,128)(2,1)S(1)}, bf16[6,1024]{1,0:T(8,128)(2,1)S(1)}, u32[]{:S(2)}, u32[]{:S(2)}) %collective-permute-start.2) | collective-permute-done | bytes 12320 | tf_op jit(solution)/shard_map/ppermute | solution.py:32
  292.2 1.9 collective-permute-start.3
  295.1 4.0 %collective-permute-done.3 = bf16[6,1024]{1,0:T(8,128)(2,1)S(1)} collective-permute-done((bf16[6,1024]{1,0:T(8,128)(2,1)S(1)}, bf16[6,1024]{1,0:T(8,128)(2,1)S(1)}, u32[]{:S(2)}, u32[]{:S(2)}) %collective-permute-start.3) | collective-permute-done | bytes 12320 | tf_op jit(solution)/shard_map/ppermute | solution.py:32
  304.7 2.2 concatenate.111
  306.9 2.1 fusion
  (70 shorter events, 8.5 us)
Async XLA Ops:
  6.5 231.6 %copy-start = (bf16[384,3072]{1,0:T(8,128)(2,1)S(1)}, bf16[384,3072]{1,0:T(8,128)(2,1)}, u32[]{:S(2)}) copy-start(bf16[384,3072]{1,0:T(8,128)(2,1)} %param.17) | copy-start | bytes 7077892
  6.5 96.7 %all-gather.3.cloned.1.call-start = ((), (), s32[]{:S(2)}) async-start(), calls=%async_computation.1 | async-start | bytes 12779520 | tf_op jit(solution)/shard_map/all_gather | solution.py:94
  8.5 188.1 %all-gather.5.cloned.1.call-start = ((), (), s32[]{:S(2)}) async-start(), calls=%async_computation.2 | async-start | bytes 12779520 | tf_op jit(solution)/shard_map/all_gather | solution.py:95
  9.2 259.2 %reduce-scatter.2.cloned.1.call-start = ((), (), s32[]{:S(2)}) async-start(), calls=%async_computation.3 | async-start | bytes 1966080 | tf_op jit(solution)/shard_map/reduce_scatter | solution.py:110
  213.2 27.1 %copy-start.3 = (f32[3072]{0:T(1024)S(1)}, f32[3072]{0:T(1024)}, u32[]{:S(2)}) copy-start(f32[3072]{0:T(1024)} %param.20) | copy-start | bytes 36868
  213.2 55.2 %copy-start.1 = (bf16[64,3072]{1,0:T(8,128)(2,1)S(1)}, bf16[64,3072]{1,0:T(8,128)(2,1)}, u32[]{:S(2)}) copy-start(bf16[64,3072]{1,0:T(8,128)(2,1)} %param.16) | copy-start | bytes 1179652
  213.2 55.2 %copy-start.2 = (f32[3072]{0:T(1024)S(1)}, f32[3072]{0:T(1024)}, u32[]{:S(2)}) copy-start(f32[3072]{0:T(1024)} %param.18) | copy-start | bytes 36868
  213.2 57.7 %copy-start.4 = (bf16[3072,64]{0,1:T(8,128)(2,1)S(1)}, bf16[3072,64]{0,1:T(8,128)(2,1)}, u32[]{:S(2)}) copy-start(bf16[3072,64]{0,1:T(8,128)(2,1)} %param.21) | copy-start | bytes 1179652
  213.2 57.7 %copy-start.5 = (f32[3072]{0:T(1024)S(1)}, f32[3072]{0:T(1024)}, u32[]{:S(2)}) copy-start(f32[3072]{0:T(1024)} %param.19) | copy-start | bytes 36868
  272.8 11.1 %collective-permute-start = (bf16[1,1024]{1,0:T(2,128)(2,1)S(1)}, bf16[1,1024]{1,0:T(2,128)(2,1)S(1)}, u32[]{:S(2)}, u32[]{:S(2)}) collective-permute-start(bf16[1,1024]{1,0:T(2,128)(2,1)S(1)} %get-tuple-element.31), channel_id=1, source_target_pairs={{0,1},{1,2},{2,3},{3,4},{4,5},{5,6},{6,7},{7,8},{8,9},{9,10},{10,1... | collective-permute-start | bytes 6152 | tf_op jit(solution)/shard_map/ppermute | solution.py:20
  275.1 10.1 %collective-permute-start.1 = (bf16[1,1024]{1,0:T(2,128)(2,1)S(1)}, bf16[1,1024]{1,0:T(2,128)(2,1)S(1)}, u32[]{:S(2)}, u32[]{:S(2)}) collective-permute-start(bf16[1,1024]{1,0:T(2,128)(2,1)S(1)} %get-tuple-element.32), channel_id=1, source_target_pairs={{1,0},{2,1},{3,2},{4,3},{5,4},{6,5},{7,6},{8,7},{9,8},{10,9},{11,1... | collective-permute-start | bytes 6152 | tf_op jit(solution)/shard_map/ppermute | solution.py:22
  285.4 6.8 %collective-permute-start.2 = (bf16[6,1024]{1,0:T(8,128)(2,1)S(1)}, bf16[6,1024]{1,0:T(8,128)(2,1)S(1)}, u32[]{:S(2)}, u32[]{:S(2)}) collective-permute-start(bf16[6,1024]{1,0:T(8,128)(2,1)S(1)} %pad_maximum_fusion.2), channel_id=1, source_target_pairs={{0,32},{4,36},{8,40},{12,44},{16,48},{20,52},{24,56},{28,60},{32,6... | collective-permute-start | bytes 36872 | tf_op jit(solution)/shard_map/ppermute | solution.py:32
  292.2 6.8 %collective-permute-start.3 = (bf16[6,1024]{1,0:T(8,128)(2,1)S(1)}, bf16[6,1024]{1,0:T(8,128)(2,1)S(1)}, u32[]{:S(2)}, u32[]{:S(2)}) collective-permute-start(bf16[6,1024]{1,0:T(8,128)(2,1)S(1)} %broadcast_select_fusion.1), channel_id=1, source_target_pairs={{0,32},{4,36},{8,40},{12,44},{16,48},{20,52},{24,56},{28,60},{32,6... | collective-permute-start | bytes 36872 | tf_op jit(solution)/shard_map/ppermute | solution.py:32
Sparse Core Ops, SparseCore 0:
  10.0 93.2 all-gather.2
  106.0 90.4 all-gather.4
  240.4 27.9 reduce-scatter.1
where the time goes:
time: 316 us
  waiting for transfers between devices  165 us (52%)
  matrix products  59.4 us (19%)
  other arithmetic  32.6 us (10%)
  local copies, waits for them, and re-layouts  30 us (9%)
  starting transfers between devices  14.9 us (5%)
  between operations  13.4 us (4%)
    all_gather x1, waiting for transfers between devices, per_device(): lax.all_gather(key_vectors, 'blk', axis=0, tiled=True)  87.7 us
    all_gather x1, waiting for transfers between devices, per_device(): lax.all_gather(values, 'blk', axis=0, tiled=True)  38.9 us
    dot_general x1, matrix products, attend_block(): jnp.einsum('qhd,khd->hqk', query_heads, key_heads, preferred_element_type...  28.9 us
    reduce_scatter x1, waiting for transfers between devices, per_device(): lax.psum_scatter(jnp.dot(attended, out_weight, preferred_element_type=jnp...  28.1 us
    reduce_sum x1, other arithmetic, attend_block(): row_total = jnp.sum(weights.astype(jnp.float32), axis=2)  25.4 us
    dot_general x1, matrix products, attend_block(): jnp.einsum('hqk,khd->hqd', weights, value_heads, preferred_element_type=j...  24.8 us
    all_gather x1, local copies, waits for them, and re-layouts, per_device(): lax.all_gather(values, 'blk', axis=0, tiled=True)  16.7 us
    ppermute x1, starting transfers between devices, padded_2(): lax.ppermute(head, axis, [((i + 1) % count, i) for i in range(ends)])  8.75 us
  transfers between devices with their start and end apart: 7, of which 6 were waited for; matrix products, arithmetic and copies ran while one was open for 20% of the time, Pallas kernels for 0%

commit v1 on v0

--- a/solution.py
+++ b/solution.py
@@ -7,6 +7,15 @@
 LC = 16
 FRAMES = 8
 PW = 32
+
+
+def _convert_stocks(s0):
+    return jnp.concatenate(
+        jax.lax.all_to_all(
+            jnp.stack(jax.lax.axis_size("blk") * [s0]), axis_name="blk", split_axis=0, concat_axis=0
+        ),
+        axis=0,
+    )
 
 
 def padded_2(cells, sides, width):
@@ -90,10 +99,7 @@
     )
     carry = attend_block(
         initial,
-        (
-            lax.all_gather(key_vectors, "blk", axis=0, tiled=True),
-            lax.all_gather(values, "blk", axis=0, tiled=True),
-        ),
+        (_convert_stocks(key_vectors), lax.all_gather(values, "blk", axis=0, tiled=True)),
         query_heads,
         query_frame,
         lookback_heads,

time: 316 us -> 545 us (1.72)
  waiting for transfers between devices: 165 us -> 346 us
  local copies, waits for them, and re-layouts: 30 us -> 66.2 us
  starting transfers between devices: 14.9 us -> 25.4 us
    all_to_all x0 -> x1, waiting for transfers between devices: none -> 304 us  [_convert_stocks(): jax.lax.all_to_all(jnp.stack(jax.lax.axis_size('blk') * [s0]), axis_name=...]
    all_gather x1 -> x0, waiting for transfers between devices: 87.7 us -> none  [per_device(): lax.all_gather(key_vectors, 'blk', axis=0, tiled=True)]
    all_gather x1, waiting for transfers between devices: 38.9 us -> 0.02 us  [per_device(): lax.all_gather(values, 'blk', axis=0, tiled=True)]
    another operation x0 -> x2, local copies, waits for them, and re-layouts: none -> 25.6 us  [the longest x1 19.6 us: attend_block(): key_heads = key_block.reshape(key_count, head_count, DH)]
    all_to_all x0 -> x1, local copies, waits for them, and re-layouts: none -> 14 us  [_convert_stocks(): jax.lax.all_to_all(jnp.stack(jax.lax.axis_size('blk') * [s0]), axis_name=...]
    all_to_all x0 -> x1, starting transfers between devices: none -> 10.5 us  [_convert_stocks(): jax.lax.all_to_all(jnp.stack(jax.lax.axis_size('blk') * [s0]), axis_name=...]
  transfers between devices with their start and end apart: 7 -> 7, of which waited for: 6 -> 5; matrix products, arithmetic and copies ran while one was open for 20% -> 17% of each run, Pallas kernels for 0% -> 0%
where the time goes in v1:
time: 545 us; the launch traced here: 544 us
  waiting for transfers between devices  346 us (63%)
  local copies, waits for them, and re-layouts  66.2 us (12%)
  matrix products  59.5 us (11%)
  other arithmetic  32.6 us (6%)
  starting transfers between devices  25.4 us (5%)
  between operations  13.7 us (3%)
    all_to_all x1, waiting for transfers between devices, _convert_stocks(): jax.lax.all_to_all(jnp.stack(jax.lax.axis_size('blk') * [s0]), axis_name=...  304 us
    reduce_scatter x1, waiting for transfers between devices, per_device(): lax.psum_scatter(jnp.dot(attended, out_weight, preferred_element_type=jnp...  32.4 us
    dot_general x1, matrix products, attend_block(): jnp.einsum('qhd,khd->hqk', query_heads, key_heads, preferred_element_type...  28.9 us
    reduce_sum x1, other arithmetic, attend_block(): row_total = jnp.sum(weights.astype(jnp.float32), axis=2)  25.4 us
    dot_general x1, matrix products, attend_block(): jnp.einsum('hqk,khd->hqd', weights, value_heads, preferred_element_type=j...  24.9 us
    another operation x1, local copies, waits for them, and re-layouts, attend_block(): key_heads = key_block.reshape(key_count, head_count, DH)  19.6 us
    all_gather x1, local copies, waits for them, and re-layouts, per_device(): lax.all_gather(values, 'blk', axis=0, tiled=True)  15.6 us
    all_to_all x1, local copies, waits for them, and re-layouts, _convert_stocks(): jax.lax.all_to_all(jnp.stack(jax.lax.axis_size('blk') * [s0]), axis_name=...  14 us
  transfers between devices with their start and end apart: 7, of which 5 were waited for; matrix products, arithmetic and copies ran while one was open for 17% of the time, Pallas kernels for 0%

profile of v1, /device:TPU:128, one launch (start us, length us, event | category | flops | bytes accessed | tf_op | source)
XLA Modules:
  0.0 543.8 jit_solution(362755646300982176)
XLA Ops:
  6.5 1.2 copy.25
  7.8 6.0 %stack.8 = bf16[64,256,384]{1,2,0:T(8,128)(2,1)} broadcast(bf16[256,384]{0,1:T(8,128)(2,1)S(1)} %copy.25), dimensions={1,2} | broadcast | bytes 12779520 | tf_op jit(solution)/shard_map/stack | solution.py:15
  13.8 10.5 %all-to-all-start = ((bf16[64,256,384]{1,2,0:T(8,128)(2,1)}), bf16[64,256,384]{1,2,0:T(8,128)(2,1)}, u32[]{:S(2)}, u32[]{:S(2)}) async-start(bf16[64,256,384]{1,2,0:T(8,128)(2,1)} %stack.8), calls=%async_computation | async-start | bytes 25165824 | tf_op jit(solution)/shard_map/all_to_all | solution.py:14
  25.4 4.4 broadcast_compare_fusion
  29.8 303.5 %all-to-all-done = bf16[64,256,384]{1,2,0:T(8,128)(2,1)} async-done(((bf16[64,256,384]{1,2,0:T(8,128)(2,1)}), bf16[64,256,384]{1,2,0:T(8,128)(2,1)}, u32[]{:S(2)}, u32[]{:S(2)}) %all-to-all-start) | async-done | bytes 12582944 | tf_op jit(solution)/shard_map/all_to_all | solution.py:14
  333.3 14.0 %copy.26 = bf16[64,256,384]{1,0,2:T(8,128)(2,1)} copy(bf16[64,256,384]{1,2,0:T(8,128)(2,1)} %all-to-all-done) | data formatting | bytes 25165824 | tf_op jit(solution)/shard_map/all_to_all | solution.py:14
  347.3 19.6 %reshape_reshape.3 = bf16[16384,3,128]{0,2,1:T(8,128)(2,1)} reshape(bf16[64,256,384]{1,0,2:T(8,128)(2,1)} %copy.26) | data formatting | bytes 25165824 | tf_op jit(solution)/shard_map/reshape;reshape | solution.py:49
  366.8 28.9 %select_reduce_fusion = (f32[3,256]{1,0:T(4,128)S(1)}, f32[3,256,16384]{2,1,0:T(8,128)}) fusion(s32[3,256]{1,0:T(4,128)S(1)} %broadcast_subtract_fusion, s32[16384]{0:T(1024)S(1)} %add_select_fusion, pred[256,16384]{1,0:T(8,128)(4,1)} %broadcast_compare_fusion, bf16[256,3,128]{0,2,1:T(8,128)(2,1)S(1)} %bitcast.82, bf16[16384,3,128]{0,2,1:T(8,128)(2,1)} %reshape_reshape.3), kind=kOutput, calls=%fused_computation.2 | convolution fusion | flops 3284139264 | bytes 67377152 | tf_op jit(solution)/shard_map/qhd,khd->hqk/dot_general | solution.py:51
  395.8 25.4 %convert_reduce_fusion = f32[3,256]{1,0:T(4,128)S(1)} fusion(f32[3,256]{1,0:T(4,128)S(1)} %broadcast_maximum_fusion, f32[3,256,16384]{2,1,0:T(8,128)} %get-tuple-element.34, s32[3,256]{1,0:T(4,128)S(1)} %broadcast_subtract_fusion, s32[16384]{0:T(1024)S(1)} %add_select_fusion, pred[256,16384]{1,0:T(8,128)(4,1)} %broadcast_compare_fusion), kind=kLoop, calls=%fused_computation | loop fusion | flops 100662528 | bytes 54600704 | tf_op jit(solution)/shard_map/reduce_sum | solution.py:64
  421.2 15.6 %copy.29 = bf16[16384,384]{0,1:T(8,128)(2,1)} copy(bf16[16384,384]{1,0:T(8,128)(2,1)} %all-gather.2.cloned.1.call-done) | data formatting | bytes 25165824 | tf_op jit(solution)/shard_map/all_gather | solution.py:102
  436.8 24.9 %fusion.2 = bf16[256,3,128]{0,2,1:T(8,128)(2,1)S(1)} fusion(bf16[16384,3,128]{0,2,1:T(8,128)(2,1)} %bitcast.52, f32[256,3]{0,1:T(4,128)S(1)} %bitcast.84, f32[3,256,16384]{2,1,0:T(8,128)} %get-tuple-element.34, f32[3,256]{1,0:T(4,128)S(1)} %broadcast_maximum_fusion, s32[3,256]{1,0:T(4,128)S(1)} %broadcast_subtract_fusion, s32[16384]{0:T(1024)S(1)} %add_select_fusion, ...), kind=kOutput, calls=%fused_computation.10 | convolution fusion | flops 3296919552 | bytes 67380224 | tf_op jit(solution)/shard_map/hqk,khd->hqd/dot_general | solution.py:65
  461.8 2.2 convolution_convert_fusion
  464.0 32.4 %reduce-scatter.2.cloned.1.call-done = bf16[64,3072]{1,0:T(8,128)(2,1)} async-done(((bf16[256,3072]{1,0:T(8,128)(2,1)}), bf16[64,3072]{1,0:T(8,128)(2,1)}) %reduce-scatter.2.cloned.1.call-update) | async-done | bytes 393232 | tf_op jit(solution)/shard_map/reduce_scatter | solution.py:116
  496.4 1.2 fusion.3
  497.6 1.3 multiply_reduce_fusion
  499.0 1.4 convolution_convert_fusion.1
  500.8 2.3 collective-permute-start
  503.1 8.7 %collective-permute-start.1 = (bf16[1,1024]{1,0:T(2,128)(2,1)S(1)}, bf16[1,1024]{1,0:T(2,128)(2,1)S(1)}, u32[]{:S(2)}, u32[]{:S(2)}) collective-permute-start(bf16[1,1024]{1,0:T(2,128)(2,1)S(1)} %get-tuple-element.32), channel_id=1, source_target_pairs={{1,0},{2,1},{3,2},{4,3},{5,4},{6,5},{7,6},{8,7},{9,8},{10,9},{11,1... | collective-permute-start | bytes 6152 | tf_op jit(solution)/shard_map/ppermute | solution.py:31
  513.3 1.9 collective-permute-start.2
  515.5 4.7 collective-permute-done.2
  520.2 1.9 collective-permute-start.3
  523.1 4.0 collective-permute-done.3
  532.6 2.2 concatenate.111
  534.8 2.1 fusion
  (76 shorter events, 9.7 us)
Async XLA Ops:
  6.5 455.2 %copy-start = (bf16[384,3072]{1,0:T(8,128)(2,1)S(1)}, bf16[384,3072]{1,0:T(8,128)(2,1)}, u32[]{:S(2)}) copy-start(bf16[384,3072]{1,0:T(8,128)(2,1)} %param.17) | copy-start | bytes 7077892
  7.8 17.3 %copy-start.2 = (bf16[256,384]{1,0:T(8,128)(2,1)S(1)}, bf16[256,384]{1,0:T(8,128)(2,1)}, u32[]{:S(2)}) copy-start(bf16[256,384]{1,0:T(8,128)(2,1)} %param.12) | copy-start | bytes 589828
  7.8 17.5 %copy-start.7 = (s32[12]{0:T(128)S(1)}, s32[12]{0:T(128)}, u32[]{:S(2)}) copy-start(s32[12]{0:T(128)} %param.15) | copy-start | bytes 148
  13.8 319.5 %all-to-all-start = ((bf16[64,256,384]{1,2,0:T(8,128)(2,1)}), bf16[64,256,384]{1,2,0:T(8,128)(2,1)}, u32[]{:S(2)}, u32[]{:S(2)}) async-start(bf16[64,256,384]{1,2,0:T(8,128)(2,1)} %stack.8), calls=%async_computation | async-start | bytes 25165824 | tf_op jit(solution)/shard_map/all_to_all | solution.py:14
  24.3 396.9 %all-gather.2.cloned.1.call-start = ((), (), s32[]{:S(2)}) async-start(), calls=%async_computation.2 | async-start | bytes 12779520 | tf_op jit(solution)/shard_map/all_gather | solution.py:102
  25.0 471.4 %reduce-scatter.2.cloned.1.call-start = ((), (), s32[]{:S(2)}) async-start(), calls=%async_computation.3 | async-start | bytes 1966080 | tf_op jit(solution)/shard_map/reduce_scatter | solution.py:116
  436.8 27.2 %copy-start.4 = (f32[3072]{0:T(1024)S(1)}, f32[3072]{0:T(1024)}, u32[]{:S(2)}) copy-start(f32[3072]{0:T(1024)} %param.20) | copy-start | bytes 36868
  436.8 59.6 %copy-start.1 = (bf16[64,3072]{1,0:T(8,128)(2,1)S(1)}, bf16[64,3072]{1,0:T(8,128)(2,1)}, u32[]{:S(2)}) copy-start(bf16[64,3072]{1,0:T(8,128)(2,1)} %param.16) | copy-start | bytes 1179652
  436.8 59.6 %copy-start.3 = (f32[3072]{0:T(1024)S(1)}, f32[3072]{0:T(1024)}, u32[]{:S(2)}) copy-start(f32[3072]{0:T(1024)} %param.18) | copy-start | bytes 36868
  436.8 62.1 %copy-start.5 = (bf16[3072,64]{0,1:T(8,128)(2,1)S(1)}, bf16[3072,64]{0,1:T(8,128)(2,1)}, u32[]{:S(2)}) copy-start(bf16[3072,64]{0,1:T(8,128)(2,1)} %param.21) | copy-start | bytes 1179652
  436.8 62.1 %copy-start.6 = (f32[3072]{0:T(1024)S(1)}, f32[3072]{0:T(1024)}, u32[]{:S(2)}) copy-start(f32[3072]{0:T(1024)} %param.19) | copy-start | bytes 36868
  500.8 11.1 %collective-permute-start = (bf16[1,1024]{1,0:T(2,128)(2,1)S(1)}, bf16[1,1024]{1,0:T(2,128)(2,1)S(1)}, u32[]{:S(2)}, u32[]{:S(2)}) collective-permute-start(bf16[1,1024]{1,0:T(2,128)(2,1)S(1)} %get-tuple-element.31), channel_id=1, source_target_pairs={{0,1},{1,2},{2,3},{3,4},{4,5},{5,6},{6,7},{7,8},{8,9},{9,10},{10,1... | collective-permute-start | bytes 6152 | tf_op jit(solution)/shard_map/ppermute | solution.py:29
  503.1 10.1 %collective-permute-start.1 = (bf16[1,1024]{1,0:T(2,128)(2,1)S(1)}, bf16[1,1024]{1,0:T(2,128)(2,1)S(1)}, u32[]{:S(2)}, u32[]{:S(2)}) collective-permute-start(bf16[1,1024]{1,0:T(2,128)(2,1)S(1)} %get-tuple-element.32), channel_id=1, source_target_pairs={{1,0},{2,1},{3,2},{4,3},{5,4},{6,5},{7,6},{8,7},{9,8},{10,9},{11,1... | collective-permute-start | bytes 6152 | tf_op jit(solution)/shard_map/ppermute | solution.py:31
  513.3 6.8 %collective-permute-start.2 = (bf16[6,1024]{1,0:T(8,128)(2,1)S(1)}, bf16[6,1024]{1,0:T(8,128)(2,1)S(1)}, u32[]{:S(2)}, u32[]{:S(2)}) collective-permute-start(bf16[6,1024]{1,0:T(8,128)(2,1)S(1)} %pad_maximum_fusion.2), channel_id=1, source_target_pairs={{0,32},{4,36},{8,40},{12,44},{16,48},{20,52},{24,56},{28,60},{32,6... | collective-permute-start | bytes 36872 | tf_op jit(solution)/shard_map/ppermute | solution.py:41
  520.2 6.8 %collective-permute-start.3 = (bf16[6,1024]{1,0:T(8,128)(2,1)S(1)}, bf16[6,1024]{1,0:T(8,128)(2,1)S(1)}, u32[]{:S(2)}, u32[]{:S(2)}) collective-permute-start(bf16[6,1024]{1,0:T(8,128)(2,1)S(1)} %broadcast_select_fusion.1), channel_id=1, source_target_pairs={{0,32},{4,36},{8,40},{12,44},{16,48},{20,52},{24,56},{28,60},{32,6... | collective-permute-start | bytes 36872 | tf_op jit(solution)/shard_map/ppermute | solution.py:41
Sparse Core Ops, SparseCore 0:
  27.8 204.4 all-gather.1
  464.1 32.2 reduce-scatter.1
